TPU v7x, 512 devices: a whole 4x8x8 slice. The times are simulated.
512 devices in a mesh: ctx: 32 (over z, x), tp: 16 (over y, core).
Axes of the slice: x: 4, y: 8, z: 8, core: 2. Of those that a mesh axis runs over, the one named last changes fastest.
Arguments:
- hidden: bfloat16 [8192, 2048], P(('ctx', 'tp')), may hold values from -14 to 14
- in_weight: bfloat16 [2048, 2, 4096], P(None, None, 'tp'), may hold values from -0.125 to 0.125
- step_weight: bfloat16 [2048, 64], P(None, 'tp'), may hold values from -0.125 to 0.125
- group_weight: bfloat16 [256, 4, 2048], P('tp'), may hold values from -0.125 to 0.125
- conv_inner: float32 [4, 4096], P(None, 'tp'), may hold values from -3 to 3
- inner_bias: float32 [4096], P('tp'), may hold values from -2.5 to 2.5
- conv_group: float32 [4, 1024], replicated, may hold values from -3 to 3
- group_bias: float32 [1024], replicated, may hold values from -2.5 to 2.5
- step_bias: float32 [64], P('tp'), may hold values from -9.5 to 0
- log_rate: float32 [64], P('tp'), may hold values from -2.5 to -0.5
- skip_weight: float32 [64], P('tp'), may hold values from 0.25 to 1
- norm_gain: float32 [4096], P('tp'), may hold values from 0.1 to 1.9
- out_weight: bfloat16 [4096, 2048], P('tp'), may hold values from -0.09375 to 0.09375
Outputs:
- mixed: bfloat16 [8192, 2048], P(('ctx', 'tp'))
All inputs are finite; a program needn't handle non-finite values.
Results may differ from a plain program's by a relative error of at most 0.024.
Values may be sent and summed in bfloat16 or wider, within the bound.
No kernel may reach another device: no remote copies, remote signals or barrier semaphores. Data moves between devices by JAX's collectives and lax.ppermute only.
A program may use at most 64 MiB of HBM per device.

v0:
```python
import jax
import jax.numpy as jnp
from jax import lax
from jax.sharding import PartitionSpec as P

HEADS = 64
HEAD_DIM = 64
STATE = 128
GROUPS = 4
BLOCK = 256
KERNEL = 4


def shifted(x, axis, by):
    peers = lax.axis_size(axis)
    pairs = [(i, i + by) for i in range(peers) if 0 <= i + by < peers]
    return lax.ppermute(x, axis, pairs)


def entering(x, axis, combine, identity):
    peers, place = (lax.axis_size(axis), lax.axis_index(axis))
    everything = jax.tree.map(lambda part: lax.all_gather(part, axis), x)
    start = jax.tree.map(
        lambda part, zero: jnp.broadcast_to(jnp.asarray(zero, part.dtype), part.shape), x, identity
    )

    def turn(k, before):
        reached = k < place
        new = combine(before, jax.tree.map(lambda part: part[k], everything))
        return jax.tree.map(lambda a, b: jnp.where(reached, a, b), new, before)

    return lax.fori_loop(0, peers, turn, start)


def causal_conv(prior_rows, raw_rows, conv_weight, conv_bias):
    joined = jnp.concatenate([prior_rows, raw_rows], axis=0).astype(jnp.float32)
    length = raw_rows.shape[0]
    running = jnp.broadcast_to(conv_bias[None, :], raw_rows.shape)
    for offset in range(conv_weight.shape[0]):
        running = running + conv_weight[offset][None, :] * joined[offset : offset + length]
    return jax.nn.silu(running).astype(jnp.bfloat16)


def combine_states(earlier, latter):
    return (earlier[0] * latter[0], latter[0][:, None, None] * earlier[1] + latter[1])


def body(
    hidden,
    in_weight,
    step_weight,
    group_weight,
    conv_inner,
    inner_bias,
    conv_group,
    group_bias,
    step_bias,
    log_rate,
    skip_weight,
    norm_gain,
    out_weight,
):
    heads_dev = log_rate.shape[0]
    inner_dev = in_weight.shape[2]
    group_cols = 2 * STATE
    group_index = lax.axis_index("tp") * heads_dev // (HEADS // GROUPS)
    zx_weight = in_weight.reshape(in_weight.shape[0], 2 * inner_dev)
    full_weight = lax.all_gather(group_weight, "tp", axis=0, tiled=True)
    map_weight = lax.dynamic_slice_in_dim(full_weight, group_index, 1, 1)[:, 0, :]
    shard_rows = lax.all_gather(hidden, "tp", axis=0, tiled=True)
    projected = jnp.concatenate(
        [
            jnp.dot(shard_rows, zx_weight, preferred_element_type=jnp.float32),
            lax.dot_general(
                shard_rows, map_weight, (((1,), (1,)), ((), ())), preferred_element_type=jnp.float32
            ),
            jnp.dot(shard_rows, step_weight, preferred_element_type=jnp.float32),
        ],
        axis=1,
    ).astype(jnp.bfloat16)
    gate_raw = projected[:, :inner_dev]
    inner_raw = projected[:, inner_dev : 2 * inner_dev]
    map_part = projected[:, 2 * inner_dev : projected.shape[1] - heads_dev]
    step_raw = projected[:, projected.shape[1] - heads_dev :]
    border_rows = KERNEL - 1
    length = inner_raw.shape[0]
    inner_prior, map_prior = shifted(
        (inner_raw[length - border_rows :], map_part[length - border_rows :]), "ctx", 1
    )
    x_conv = causal_conv(inner_prior, inner_raw, conv_inner, inner_bias)
    own_taps = lax.dynamic_slice_in_dim(conv_group, group_index * group_cols, group_cols, 1)
    own_bias = lax.dynamic_slice_in_dim(group_bias, group_index * group_cols, group_cols, 0)
    maps = causal_conv(map_prior, map_part, own_taps, own_bias)
    step_size = jax.nn.softplus(step_raw.astype(jnp.float32) + step_bias[None, :])
    decay_rate = -jnp.exp(log_rate)
    blocks = length // BLOCK
    x_blocks = x_conv.reshape(blocks, BLOCK, heads_dev, HEAD_DIM)
    input_map = maps[:, :STATE].reshape(blocks, BLOCK, STATE)
    output_map = maps[:, STATE:].reshape(blocks, BLOCK, STATE)
    step_blocks = jnp.swapaxes(step_size.reshape(blocks, BLOCK, heads_dev), 1, 2)
    cumulative = jnp.cumsum(step_blocks * decay_rate[None, :, None], axis=2)
    scores = jnp.einsum("kin,kjn->kij", output_map, input_map, preferred_element_type=jnp.float32)
    causal = jnp.arange(BLOCK)[:, None] >= jnp.arange(BLOCK)[None, :]
    exponent = jnp.where(causal, cumulative[..., :, None] - cumulative[..., None, :], -jnp.inf)
    mixing = (scores[:, None] * jnp.exp(exponent) * step_blocks[..., None, :]).astype(jnp.bfloat16)
    within = jnp.einsum("khij,kjhp->kihp", mixing, x_blocks, preferred_element_type=jnp.float32)
    weight = jnp.exp(cumulative[..., BLOCK - 1 :] - cumulative) * step_blocks
    x_float = x_blocks.astype(jnp.float32)
    weighted = (x_float * jnp.swapaxes(weight, 1, 2)[..., None]).astype(jnp.bfloat16)
    block_state = jnp.einsum(
        "kjhp,kjn->khpn", weighted, input_map, preferred_element_type=jnp.float32
    )
    block_decay = jnp.exp(cumulative[..., BLOCK - 1])

    def advance(carry, item):
        running, product = carry
        block_stop_index, state_here = item
        return (
            (block_stop_index[:, None, None] * running + state_here, product * block_stop_index),
            (running, product),
        )

    empty_state = jnp.zeros((heads_dev, HEAD_DIM, STATE), jnp.float32)
    (dev_state, dev_decay), (local_starts, prefixes) = lax.scan(
        advance, (empty_state, jnp.ones((heads_dev,), jnp.float32)), (block_decay, block_state)
    )
    decay_in, incoming = entering(
        (dev_decay, dev_state),
        "ctx",
        combine_states,
        (jnp.ones_like(dev_decay), jnp.zeros_like(dev_state)),
    )
    starting = local_starts + prefixes[:, :, None, None] * incoming[None]
    carried = jnp.einsum(
        "kin,khpn->kihp",
        output_map,
        starting.astype(jnp.bfloat16),
        preferred_element_type=jnp.float32,
    )
    carried = carried * jnp.swapaxes(jnp.exp(cumulative), 1, 2)[..., None]
    result_heads = within + carried + skip_weight[None, None, :, None] * x_float
    result_heads = result_heads.reshape(length, inner_dev)
    gated = result_heads * jax.nn.silu(gate_raw.astype(jnp.float32))
    squares = jnp.sum(gated * gated, axis=1)
    own_slot = (jnp.arange(GROUPS) == group_index)[:, None]
    group_sums = lax.psum(jnp.where(own_slot, squares[None, :], 0.0), "tp")
    own_total = jnp.sum(jnp.where(own_slot, group_sums, 0.0), axis=0)
    inverse = lax.rsqrt(own_total / (HEADS * HEAD_DIM // GROUPS) + 1e-05)
    normed = (gated * inverse[:, None] * norm_gain[None, :]).astype(jnp.bfloat16)
    mixed = lax.psum_scatter(
        jnp.dot(normed, out_weight, preferred_element_type=jnp.float32),
        "tp",
        scatter_dimension=0,
        tiled=True,
    )
    return mixed.astype(jnp.bfloat16)


def solution(mesh):
    placed = (
        P(("ctx", "tp"), None),
        P(None, None, "tp"),
        P(None, "tp"),
        P("tp", None, None),
        P(None, "tp"),
        P("tp"),
        P(),
        P(),
        P("tp"),
        P("tp"),
        P("tp"),
        P("tp"),
        P("tp", None),
    )
    return jax.shard_map(
        body, mesh=mesh, in_specs=placed, out_specs=P(("ctx", "tp"), None), check_vma=False
    )
```

profile of v0, /device:TPU:27, one launch (start us, length us, event | category | flops | bytes accessed | tf_op | source)
XLA Modules:
  0.0 323.9 jit_solution(4867282855328708421)
XLA Ops:
  6.5 0.7 all-gather.6.cloned.1.call-update
  7.3 1.8 copy.45
  9.3 2.1 copy.56
  11.3 0.8 dynamic_slice.29
  12.1 0.9 constant_dynamic-slice_fusion
  13.1 41.7 %all-gather.6.cloned.1.call-done = bf16[256,2048]{1,0:T(8,128)(2,1)} async-done(((bf16[16,2048]{1,0:T(8,128)(2,1)}), bf16[256,2048]{1,0:T(8,128)(2,1)}) %all-gather.6.cloned.1.call-update) | async-done | bytes 1048592 | tf_op jit(solution)/shard_map/all_gather | solution.py:70
  54.8 1.6 bitcast_multiply_fusion.1
  56.4 1.2 reduce-window.6
  58.1 1.9 convolution_convert_fusion
  60.1 3.1 collective-permute-start
  63.2 0.2 slice_reduce_fusion
  63.5 0.1 copy.50
  63.6 0.8 collective-permute-done
  64.4 35.8 %all-gather.8.cloned.1.call-done = bf16[256,4,2048]{2,0,1:T(8,128)(2,1)} async-done(((bf16[16,4,2048]{2,0,1:T(8,128)(2,1)}), bf16[256,4,2048]{2,0,1:T(8,128)(2,1)}) %all-gather.8.cloned.1.call-update) | async-done | bytes 4194320 | tf_op jit(solution)/shard_map/all_gather | solution.py:68
  100.3 2.0 fusion.4
  102.3 3.1 collective-permute-start.1
  105.4 0.2 multiply_convert_fusion.3
  105.7 0.9 collective-permute-done.1
  106.6 0.2 multiply_convert_fusion.4
  106.8 0.8 convolution_add_fusion
  107.9 34.2 %all-gather = f32[32,4,1]{1,2,0:T(1,128)S(1)} all-gather(f32[1,4,1]{1,2,0:T(1,128)S(1)} %copy.48), channel_id=2, replica_groups=mesh['ctx'=32,'tp'=16] {'ctx'}, dimensions={0}, use_global_device_ids=true | all-gather | bytes 528 | tf_op jit(solution)/shard_map/all_gather | solution.py:22
  142.4 0.2 fusion.34
  142.6 49.1 %all-gather.10.cloned.1.call-done = f32[128,64,128]{2,1,0:T(8,128)} async-done(((f32[4,64,128]{2,1,0:T(8,128)}), f32[128,64,128]{2,1,0:T(8,128)}) %all-gather.10.cloned.1.call-update) | async-done | bytes 4194320 | tf_op jit(solution)/shard_map/all_gather | solution.py:22
  191.7 33.1 %while.9 = (s32[]{:T(128)}, f32[4,64,128]{2,1,0:T(8,128)S(1)}, s32[]{:T(128)}, f32[32,4]{1,0:T(8,128)S(1)}, f32[32,4,64,128]{3,2,1,0:T(8,128)}, /*index=5*/s32[]{:T(128)}, s32[]{:T(128)}) while((s32[]{:T(128)}, f32[4,64,128]{2,1,0:T(8,128)S(1)}, s32[]{:T(128)}, f32[32,4]{1,0:T(8,128)S(1)}, f32[32,4,64,128]{3,2,1,0:T(8,128)}, ...), condition=%wide.region_3.4_spmd.clone, body=%wide.region_2.3_spmd.clone.sunk | while | flops 131076 | bytes 393369 | solution.py:32
  191.7 1.0 fusion.52
  192.7 1.0 fusion.52
  193.8 1.0 fusion.52
  194.8 1.0 fusion.52
  195.8 1.0 fusion.52
  196.9 1.0 fusion.52
  197.9 1.0 fusion.52
  198.9 1.0 fusion.52
  200.0 1.0 fusion.52
  201.0 1.0 fusion.52
  202.0 1.0 fusion.52
  203.1 1.0 fusion.52
  204.1 1.0 fusion.52
  205.1 1.0 fusion.52
  206.2 1.0 fusion.52
  207.2 1.0 fusion.52
  208.2 1.0 fusion.52
  209.3 1.0 fusion.52
  210.3 1.0 fusion.52
  211.3 1.0 fusion.52
  212.4 1.0 fusion.52
  213.4 1.0 fusion.52
  214.5 1.0 fusion.52
  215.5 1.0 fusion.52
  216.5 1.0 fusion.52
  217.6 1.0 fusion.52
  218.6 1.0 fusion.52
  219.6 1.0 fusion.52
  220.7 1.0 fusion.52
  221.7 1.0 fusion.52
  222.7 1.0 fusion.52
  223.8 1.0 fusion.52
  224.8 0.2 fusion.1
  225.0 0.5 fusion.3
  225.5 0.1 copy.54
  225.6 0.2 multiply_reduce_fusion
  225.8 26.8 %psum.7 = f32[4,256]{1,0:T(4,128)S(1)} all-reduce(f32[4,256]{1,0:T(4,128)S(1)} %broadcast_select_fusion), channel_id=1, replica_groups=mesh['ctx'=32,'tp'=16] {'tp'}, use_global_device_ids=true, to_apply=%region_5.6 | all-reduce | flops 1024 | bytes 8192 | tf_op jit(solution)/shard_map/psum | solution.py:146
  252.8 1.8 fusion.27
  254.7 61.1 %reduce-scatter.2.cloned.1.call-done = f32[16,2048]{1,0:T(8,128)} async-done(((f32[256,2048]{1,0:T(8,128)}), f32[16,2048]{1,0:T(8,128)}) %reduce-scatter.2.cloned.1.call-update) | async-done | bytes 131088 | tf_op jit(solution)/shard_map/reduce_scatter | solution.py:150
  315.8 1.5 convert_element_type.77
  (87 shorter events, 1.8 us)
Async XLA Ops:
  6.5 246.2 %copy-start = (bf16[256,2048]{1,0:T(8,128)(2,1)S(1)}, bf16[256,2048]{1,0:T(8,128)(2,1)}, u32[]{:S(2)}) copy-start(bf16[256,2048]{1,0:T(8,128)(2,1)} %param.27) | copy-start | bytes 3145732
  6.5 48.3 %all-gather.6.cloned.1.call-start = ((), (), s32[]{:S(2)}) async-start(), calls=%async_computation.1 | async-start | bytes 1114112 | tf_op jit(solution)/shard_map/all_gather | solution.py:70
  7.3 93.0 %all-gather.8.cloned.1.call-start = ((), (), s32[]{:S(2)}) async-start(), calls=%async_computation.2 | async-start | bytes 4456448 | tf_op jit(solution)/shard_map/all_gather | solution.py:68
  9.2 182.5 %all-gather.10.cloned.1.call-start = ((), (), s32[]{:S(2)}) async-start(), calls=%async_computation.4 | async-start | bytes 4325376 | tf_op jit(solution)/shard_map/all_gather | solution.py:22
  9.2 3.8 %copy-start.5 = (f32[4]{0:T(128)S(1)}, f32[4]{0:T(128)}, u32[]{:S(2)}) copy-start(f32[4]{0:T(128)} %param.24) | copy-start | bytes 52
  9.2 3.8 %copy-start.1 = (f32[4,256]{1,0:T(4,128)S(1)}, f32[4,256]{1,0:T(4,128)}, u32[]{:S(2)}) copy-start(f32[4,256]{1,0:T(4,128)} %param.19) | copy-start | bytes 12292
  9.3 45.5 %copy-start.4 = (bf16[2048,4]{0,1:T(4,128)(2,1)S(1)}, bf16[2048,4]{0,1:T(4,128)(2,1)}, u32[]{:S(2)}) copy-start(bf16[2048,4]{0,1:T(4,128)(2,1)} %param.17) | copy-start | bytes 49156
  9.3 45.5 %copy-start.6 = (f32[4]{0:T(128)S(1)}, f32[4]{0:T(128)}, u32[]{:S(2)}) copy-start(f32[4]{0:T(128)} %param.23) | copy-start | bytes 52
  60.0 45.4 %copy-start.3 = (f32[256]{0:T(256)S(1)}, f32[256]{0:T(256)}, u32[]{:S(2)}) copy-start(f32[256]{0:T(256)} %param.20) | copy-start | bytes 3076
  60.1 4.3 %collective-permute-start = (bf16[3,256]{1,0:T(4,128)(2,1)S(1)}, bf16[3,256]{1,0:T(4,128)(2,1)S(1)}, u32[]{:S(2)}, u32[]{:S(2)}) collective-permute-start(bf16[3,256]{1,0:T(4,128)(2,1)S(1)} %slice.112), channel_id=1, source_target_pairs={{0,16},{16,32},{32,48},{48,64},{64,80},{80,96},{96,112},{112,128},... | collective-permute-start | bytes 4616 | tf_op jit(solution)/shard_map/ppermute | solution.py:17
  102.3 4.3 %collective-permute-start.1 = (bf16[3,256]{1,0:T(4,128)(2,1)S(1)}, bf16[3,256]{1,0:T(4,128)(2,1)S(1)}, u32[]{:S(2)}, u32[]{:S(2)}) collective-permute-start(bf16[3,256]{1,0:T(4,128)(2,1)S(1)} %slice.118), channel_id=1, source_target_pairs={{0,16},{16,32},{32,48},{48,64},{64,80},{80,96},{96,112},{112,128},... | collective-permute-start | bytes 4616 | tf_op jit(solution)/shard_map/ppermute | solution.py:17
  106.8 118.1 %copy-start.7 = (f32[4]{0:T(128)S(1)}, f32[4]{0:T(128)}, u32[]{:S(2)}) copy-start(f32[4]{0:T(128)} %param.25) | copy-start | bytes 52
  107.7 208.1 %reduce-scatter.2.cloned.1.call-start = ((), (), s32[]{:S(2)}) async-start(), calls=%async_computation.3 | async-start | bytes 2228224 | tf_op jit(solution)/shard_map/reduce_scatter | solution.py:150
  224.8 28.0 %copy-start.2 = (f32[256]{0:T(256)S(1)}, f32[256]{0:T(256)}, u32[]{:S(2)}) copy-start(f32[256]{0:T(256)} %param.26) | copy-start | bytes 3076
Sparse Core Ops, SparseCore 0:
  9.5 45.2 all-gather.5
  56.9 43.2 all-gather.7
  107.8 83.8 all-gather.9
  254.8 60.9 reduce-scatter.1
where the time goes:
time: 325 us; the launch traced here: 324 us
  waiting for transfers between devices  190 us (58%)
  blocking collectives  61.1 us (19%)
  other arithmetic  35.5 us (11%)
  between operations  13.5 us (4%)
  matrix products  9.08 us (3%)
  local copies, waits for them, and re-layouts  7.25 us (2%)
  starting transfers between devices  6.32 us (2%)
    reduce_scatter x1, waiting for transfers between devices, body(): lax.psum_scatter(jnp.dot(normed, out_weight, preferred_element_type=jnp.f...  61.1 us
    all_gather x1, waiting for transfers between devices, entering(): everything = jax.tree.map(lambda part: lax.all_gather(part, axis), x)  49.1 us
    all_gather x1, waiting for transfers between devices, body(): shard_rows = lax.all_gather(hidden, 'tp', axis=0, tiled=True)  41.7 us
    all_gather x1, waiting for transfers between devices, body(): full_weight = lax.all_gather(group_weight, 'tp', axis=0, tiled=True)  35.8 us
    all_gather x1, blocking collectives, entering(): everything = jax.tree.map(lambda part: lax.all_gather(part, axis), x)  34.2 us
    select_n x32, other arithmetic, turn(): return jax.tree.map(lambda a, b: jnp.where(reached, a, b), new, before)  31.8 us
    psum x1, blocking collectives, body(): group_sums = lax.psum(jnp.where(own_slot, squares[None, :], 0.0), 'tp')  26.8 us
  transfers between devices with their start and end apart: 6, of which 6 were waited for; matrix products, arithmetic and copies ran while one was open for 4% of the time, Pallas kernels for 0%

commit v1 on v0

--- a/solution.py
+++ b/solution.py
@@ -9,6 +9,14 @@
 GROUPS = 4
 BLOCK = 256
 KERNEL = 4
+
+
+def _replace_plate(xin):
+    part_next = jnp.stack([xin for _ in range(lax.psum(1, axis_name="tp"))])
+    block_now = jnp.concatenate(
+        lax.all_to_all(part_next, axis_name="tp", split_axis=0, concat_axis=0), 0
+    )
+    return block_now
 
 
 def shifted(x, axis, by):
@@ -65,7 +73,7 @@
     group_cols = 2 * STATE
     group_index = lax.axis_index("tp") * heads_dev // (HEADS // GROUPS)
     zx_weight = in_weight.reshape(in_weight.shape[0], 2 * inner_dev)
-    full_weight = lax.all_gather(group_weight, "tp", axis=0, tiled=True)
+    full_weight = _replace_plate(group_weight)
     map_weight = lax.dynamic_slice_in_dim(full_weight, group_index, 1, 1)[:, 0, :]
     shard_rows = lax.all_gather(hidden, "tp", axis=0, tiled=True)
     projected = jnp.concatenate(

time: 325 us -> 345 us (1.062)
  the two profiles are of different devices: /device:TPU:27 before, /device:TPU:25 now
where the time goes in v1:
time: 345 us; the launch traced here: 344 us
  waiting for transfers between devices  196 us (57%)
  blocking collectives  65.5 us (19%)
  other arithmetic  35.5 us (10%)
  between operations  13.5 us (4%)
  starting transfers between devices  13.4 us (4%)
  local copies, waits for them, and re-layouts  11.4 us (3%)
  matrix products  8.23 us (2%)
    all_gather x1, waiting for transfers between devices, body(): shard_rows = lax.all_gather(hidden, 'tp', axis=0, tiled=True)  61.7 us
    reduce_scatter x1, waiting for transfers between devices, body(): lax.psum_scatter(jnp.dot(normed, out_weight, preferred_element_type=jnp.f...  59.9 us
    all_gather x1, waiting for transfers between devices, entering(): everything = jax.tree.map(lambda part: lax.all_gather(part, axis), x)  48.8 us
    all_gather x1, blocking collectives, entering(): everything = jax.tree.map(lambda part: lax.all_gather(part, axis), x)  38.8 us
    select_n x32, other arithmetic, turn(): return jax.tree.map(lambda a, b: jnp.where(reached, a, b), new, before)  31.8 us
    psum x1, blocking collectives, body(): group_sums = lax.psum(jnp.where(own_slot, squares[None, :], 0.0), 'tp')  26.7 us
    all_to_all x1, waiting for transfers between devices, _replace_plate(): lax.all_to_all(part_next, axis_name='tp', split_axis=0, concat_axis=0)  24.1 us
    all_to_all x1, starting transfers between devices, _replace_plate(): lax.all_to_all(part_next, axis_name='tp', split_axis=0, concat_axis=0)  10.3 us
  transfers between devices with their start and end apart: 6, of which 6 were waited for; matrix products, arithmetic and copies ran while one was open for 3% of the time, Pallas kernels for 0%

profile of v1, /device:TPU:25, one launch (start us, length us, event | category | flops | bytes accessed | tf_op | source)
XLA Modules:
  0.0 344.3 jit_solution(17524797760392816426)
XLA Ops:
  6.5 1.2 copy.46
  7.7 2.5 stack.2
  10.2 10.3 %all-to-all-start = ((bf16[16,16,4,2048]{3,1,2,0:T(8,128)(2,1)}), bf16[16,16,4,2048]{3,1,2,0:T(8,128)(2,1)}, u32[]{:S(2)}, u32[]{:S(2)}) async-start(bf16[16,16,4,2048]{3,1,2,0:T(8,128)(2,1)} %stack.2), calls=%async_computation | async-start | bytes 8388608 | tf_op jit(solution)/shard_map/all_to_all | solution.py:17
  20.6 0.7 all-gather.5.cloned.1.call-update
  21.4 1.8 copy.58
  23.2 0.8 dynamic_slice.29
  24.0 0.9 constant_dynamic-slice_fusion
  24.9 61.7 %all-gather.5.cloned.1.call-done = bf16[256,2048]{1,0:T(8,128)(2,1)} async-done(((bf16[16,2048]{1,0:T(8,128)(2,1)}), bf16[256,2048]{1,0:T(8,128)(2,1)}) %all-gather.5.cloned.1.call-update) | async-done | bytes 1048592 | tf_op jit(solution)/shard_map/all_gather | solution.py:78
  86.6 1.6 bitcast_multiply_fusion.1
  88.3 1.2 reduce-window.6
  89.9 2.6 convolution_convert_fusion
  92.6 1.7 collective-permute-start
  94.3 0.2 slice_reduce_fusion
  94.7 0.2 collective-permute-done
  95.0 24.1 %all-to-all-done = bf16[16,16,4,2048]{3,1,2,0:T(8,128)(2,1)} async-done(((bf16[16,16,4,2048]{3,1,2,0:T(8,128)(2,1)}), bf16[16,16,4,2048]{3,1,2,0:T(8,128)(2,1)}, u32[]{:S(2)}, u32[]{:S(2)}) %all-to-all-start) | async-done | bytes 4194336 | tf_op jit(solution)/shard_map/all_to_all | solution.py:17
  119.2 2.5 copy.47
  121.7 0.5 fusion.4
  122.2 1.3 collective-permute-start.1
  123.5 0.2 multiply_convert_fusion.3
  123.8 0.4 collective-permute-done.1
  124.2 0.2 multiply_convert_fusion.4
  124.4 0.8 convolution_add_fusion
  125.5 38.8 %all-gather = f32[32,4,1]{1,2,0:T(1,128)S(1)} all-gather(f32[1,4,1]{1,2,0:T(1,128)S(1)} %copy.50), channel_id=2, replica_groups=mesh['ctx'=32,'tp'=16] {'ctx'}, dimensions={0}, use_global_device_ids=true | all-gather | bytes 528 | tf_op jit(solution)/shard_map/all_gather | solution.py:30
  164.6 0.2 fusion.34
  164.8 48.8 %all-gather.7.cloned.1.call-done = f32[128,64,128]{2,1,0:T(8,128)} async-done(((f32[4,64,128]{2,1,0:T(8,128)}), f32[128,64,128]{2,1,0:T(8,128)}) %all-gather.7.cloned.1.call-update) | async-done | bytes 4194320 | tf_op jit(solution)/shard_map/all_gather | solution.py:30
  213.6 33.0 %while.9 = (s32[]{:T(128)}, f32[4,64,128]{2,1,0:T(8,128)S(1)}, s32[]{:T(128)}, f32[32,4]{1,0:T(8,128)S(1)}, f32[32,4,64,128]{3,2,1,0:T(8,128)}, /*index=5*/s32[]{:T(128)}, s32[]{:T(128)}) while((s32[]{:T(128)}, f32[4,64,128]{2,1,0:T(8,128)S(1)}, s32[]{:T(128)}, f32[32,4]{1,0:T(8,128)S(1)}, f32[32,4,64,128]{3,2,1,0:T(8,128)}, ...), condition=%wide.region_3.4_spmd.clone, body=%wide.region_2.3_spmd.clone.sunk | while | flops 131076 | bytes 393369 | solution.py:40
  213.6 1.0 fusion.52
  214.6 1.0 fusion.52
  215.6 1.0 fusion.52
  216.7 1.0 fusion.52
  217.7 1.0 fusion.52
  218.7 1.0 fusion.52
  219.8 1.0 fusion.52
  220.8 1.0 fusion.52
  221.8 1.0 fusion.52
  222.9 1.0 fusion.52
  223.9 1.0 fusion.52
  224.9 1.0 fusion.52
  226.0 1.0 fusion.52
  227.0 1.0 fusion.52
  228.0 1.0 fusion.52
  229.1 1.0 fusion.52
  230.1 1.0 fusion.52
  231.1 1.0 fusion.52
  232.2 1.0 fusion.52
  233.2 1.0 fusion.52
  234.2 1.0 fusion.52
  235.3 1.0 fusion.52
  236.3 1.0 fusion.52
  237.3 1.0 fusion.52
  238.4 1.0 fusion.52
  239.4 1.0 fusion.52
  240.4 1.0 fusion.52
  241.5 1.0 fusion.52
  242.5 1.0 fusion.52
  243.5 1.0 fusion.52
  244.6 1.0 fusion.52
  245.6 1.0 fusion.52
  246.6 0.2 fusion.1
  246.8 0.5 fusion.3
  247.7 26.7 %psum.7 = f32[4,256]{1,0:T(4,128)S(1)} all-reduce(f32[4,256]{1,0:T(4,128)S(1)} %broadcast_select_fusion), channel_id=1, replica_groups=mesh['ctx'=32,'tp'=16] {'tp'}, use_global_device_ids=true, to_apply=%region_5.6 | all-reduce | flops 1024 | bytes 8192 | tf_op jit(solution)/shard_map/psum | solution.py:154
  274.5 1.8 fusion.27
  276.4 59.9 %reduce-scatter.2.cloned.1.call-done = f32[16,2048]{1,0:T(8,128)} async-done(((f32[256,2048]{1,0:T(8,128)}), f32[16,2048]{1,0:T(8,128)}) %reduce-scatter.2.cloned.1.call-update) | async-done | bytes 131088 | tf_op jit(solution)/shard_map/reduce_scatter | solution.py:158
  336.2 1.5 convert_element_type.77
  (92 shorter events, 2.3 us)
Async XLA Ops:
  6.5 268.0 %copy-start = (bf16[256,2048]{1,0:T(8,128)(2,1)S(1)}, bf16[256,2048]{1,0:T(8,128)(2,1)}, u32[]{:S(2)}) copy-start(bf16[256,2048]{1,0:T(8,128)(2,1)} %param.27) | copy-start | bytes 3145732
  10.2 11.1 %copy-start.1 = (bf16[2048,2,256]{2,1,0:T(2,128)(2,1)S(1)}, bf16[2048,2,256]{2,1,0:T(2,128)(2,1)}, u32[]{:S(2)}) copy-start(bf16[2048,2,256]{2,1,0:T(2,128)(2,1)} %param.16) | copy-start | bytes 6291460
  10.2 108.9 %all-to-all-start = ((bf16[16,16,4,2048]{3,1,2,0:T(8,128)(2,1)}), bf16[16,16,4,2048]{3,1,2,0:T(8,128)(2,1)}, u32[]{:S(2)}, u32[]{:S(2)}) async-start(bf16[16,16,4,2048]{3,1,2,0:T(8,128)(2,1)} %stack.2), calls=%async_computation | async-start | bytes 8388608 | tf_op jit(solution)/shard_map/all_to_all | solution.py:17
  20.5 4.3 %copy-start.7 = (f32[4]{0:T(128)S(1)}, f32[4]{0:T(128)}, u32[]{:S(2)}) copy-start(f32[4]{0:T(128)} %param.24) | copy-start | bytes 52
  20.5 4.4 %copy-start.3 = (f32[4,256]{1,0:T(4,128)S(1)}, f32[4,256]{1,0:T(4,128)}, u32[]{:S(2)}) copy-start(f32[4,256]{1,0:T(4,128)} %param.19) | copy-start | bytes 12292
  20.5 66.1 %copy-start.6 = (bf16[2048,4]{0,1:T(4,128)(2,1)S(1)}, bf16[2048,4]{0,1:T(4,128)(2,1)}, u32[]{:S(2)}) copy-start(bf16[2048,4]{0,1:T(4,128)(2,1)} %param.17) | copy-start | bytes 49156
  20.5 66.1 %copy-start.8 = (f32[4]{0:T(128)S(1)}, f32[4]{0:T(128)}, u32[]{:S(2)}) copy-start(f32[4]{0:T(128)} %param.23) | copy-start | bytes 52
  20.6 66.1 %all-gather.5.cloned.1.call-start = ((), (), s32[]{:S(2)}) async-start(), calls=%async_computation.2 | async-start | bytes 1114112 | tf_op jit(solution)/shard_map/all_gather | solution.py:78
  21.3 192.3 %all-gather.7.cloned.1.call-start = ((), (), s32[]{:S(2)}) async-start(), calls=%async_computation.4 | async-start | bytes 4325376 | tf_op jit(solution)/shard_map/all_gather | solution.py:30
  92.6 2.4 collective-permute-start
  95.0 26.7 %copy-start.2 = (bf16[256,2048]{1,0:T(8,128)(2,1)S(1)}, bf16[256,2048]{1,0:T(8,128)(2,1)}, u32[]{:S(2)}) copy-start(bf16[256,2048]{1,0:T(8,128)(2,1)} %all-gather.5.cloned.1.call-done) | copy-start | bytes 3145732
  95.0 28.5 %copy-start.5 = (f32[256]{0:T(256)S(1)}, f32[256]{0:T(256)}, u32[]{:S(2)}) copy-start(f32[256]{0:T(256)} %param.20) | copy-start | bytes 3076
  122.2 124.7 %copy-start.9 = (f32[4]{0:T(128)S(1)}, f32[4]{0:T(128)}, u32[]{:S(2)}) copy-start(f32[4]{0:T(128)} %param.25) | copy-start | bytes 52
  122.2 2.0 collective-permute-start.1
  124.2 150.3 %copy-start.4 = (f32[256]{0:T(256)S(1)}, f32[256]{0:T(256)}, u32[]{:S(2)}) copy-start(f32[256]{0:T(256)} %param.26) | copy-start | bytes 3076
  125.3 211.0 %reduce-scatter.2.cloned.1.call-start = ((), (), s32[]{:S(2)}) async-start(), calls=%async_computation.3 | async-start | bytes 2228224 | tf_op jit(solution)/shard_map/reduce_scatter | solution.py:158
Sparse Core Ops, SparseCore 0:
  23.5 63.0 all-gather.4
  125.4 88.1 all-gather.6
  276.5 59.7 reduce-scatter.1
